TPU v7x, 32 devices: a whole 2x2x4 slice. The times are simulated.
32 devices in a mesh: clips: 2 (over y), frame: 4 (over x, core), row: 4 (over z).
Axes of the slice: x: 2, y: 2, z: 4, core: 2. Of those that a mesh axis runs over, the one named last changes fastest.
Arguments:
- frames: bfloat16 [16, 512, 640], P(('clips', 'frame'), 'row'), parts along dimension 0, may hold values from -16 to 16
- key_index: int32 [4], P('clips'), parts along dimension 0, may hold values from 0 to 7, as said below
- w_query: bfloat16 [640, 640], replicated, may hold values from -0.25 to 0.25
- w_keyval: bfloat16 [640, 1280], replicated, may hold values from -0.25 to 0.25
- w_out: bfloat16 [640, 640], replicated, may hold values from -0.25 to 0.25
- norm_gain: float32 [640], replicated, may hold values from 0.1 to 1.9
- w_first: bfloat16 [3, 640, 640], replicated, may hold values from -0.125 to 0.125
- w_second: bfloat16 [3, 640, 640], replicated, may hold values from -0.125 to 0.125
Outputs:
- edited: bfloat16 [16, 512, 640], P(('clips', 'frame'), 'row'), parts along dimension 0
There are 2 independent parts, one for each index of `clips`. A program takes and returns all parts, laid end to end along the dimension named above; an argument that names none is the same for every part. Nothing has to cross between parts.
Inputs may be any that keep to these rules, and one draw needn't show every extreme that they name: `key_index`: two different frame indices of the window, in either order; one of them is the window's last frame 8 - 1.
All inputs are finite; a program needn't handle non-finite values.
Results may differ from a plain program's by a relative error of at most 0.0067.
Values may be sent and summed in bfloat16 or wider, within the bound.
No kernel may reach another device: no remote copies, remote signals or barrier semaphores. Data moves between devices by JAX's collectives and lax.ppermute only.
A program may use at most 128 MiB of HBM per device.

v0:
```python
from functools import partial
import jax
import jax.numpy as jnp
from jax import lax
from jax.sharding import PartitionSpec as P

HEADS = 10
HEAD_DIM = 64


def from_root(value, axis, source):
    kept = jnp.where(lax.axis_index(axis) == source, value, 0).astype(value.dtype)
    return lax.psum(kept, axis)


def extended(array, sides, width):
    for axis, dim in sides:
        size, length = (lax.axis_size(axis), array.shape[dim])
        up = [(i, (i + 1) % size) for i in range(size - 1)]
        down = [(j, i) for i, j in up]
        last = lax.slice_in_dim(array, length - width, length, axis=dim)
        first = lax.slice_in_dim(array, 0, width, axis=dim)
        before = lax.ppermute(last, axis, up)
        after = lax.ppermute(first, axis, down)
        array = jnp.concatenate([before, array, after], axis=dim)
    return array


def temporal_mix(padded, weights, count):
    result = jnp.zeros((count * padded.shape[1], padded.shape[2]), jnp.float32)
    for offset in range(3):
        window = padded[offset : offset + count].reshape(-1, padded.shape[2])
        result = result + jnp.dot(window, weights[offset], preferred_element_type=jnp.float32)
    return result


def absorb_keys(query_heads, channels, state_now, kv_pieces, piece_start):
    highest, denominator, accumulated = state_now
    joined = jnp.concatenate(kv_pieces, axis=0)
    key_heads = joined[:, :channels].reshape(-1, HEADS, HEAD_DIM)
    value_heads = joined[:, channels:].reshape(-1, HEADS, HEAD_DIM)
    scores = jnp.einsum(
        "qhd,khd->hqk", query_heads, key_heads, preferred_element_type=jnp.float32
    ) * HEAD_DIM ** (-0.5)
    raised = jnp.maximum(highest, jnp.max(scores, axis=-1))
    kept_frac = jnp.exp(highest - raised)
    exponent = jnp.exp(scores - raised[:, :, None])
    denominator = jnp.sum(exponent, axis=-1)
    contrib = jnp.einsum(
        "hqk,khd->qhd",
        exponent.astype(jnp.bfloat16),
        value_heads,
        preferred_element_type=jnp.float32,
    )
    accumulated = accumulated * jnp.repeat(kept_frac.T, HEAD_DIM, axis=1) + contrib.reshape(
        contrib.shape[0], -1
    )
    return (raised, denominator, accumulated)


def shards(frames, key_index, w_query, w_keyval, w_out, norm_gain, w_first, w_second):
    frame_count, row_count, channels = frames.shape
    flattened = frames.reshape(-1, channels)
    queries = jnp.dot(flattened, w_query, preferred_element_type=jnp.float32).astype(jnp.bfloat16)
    query_heads = queries.reshape(-1, HEADS, HEAD_DIM)
    query_total = queries.shape[0]
    owners = key_index // frame_count
    chosen = frames[key_index % frame_count].reshape(-1, channels)
    keyval = jnp.dot(chosen, w_keyval, preferred_element_type=jnp.float32).astype(jnp.bfloat16)
    own_parts = (keyval[:row_count], keyval[row_count:])
    initial = (
        jnp.full((HEADS, query_total), -1e30, jnp.float32),
        jnp.zeros((HEADS, query_total), jnp.float32),
        jnp.zeros((query_total, channels), jnp.float32),
    )
    absorb = partial(absorb_keys, query_heads, channels)
    spread_parts = []
    for key_slot in range(2):
        spread_parts.append(from_root(own_parts[key_slot], "frame", owners[key_slot]))
    final = absorb(
        initial,
        (
            lax.all_gather(spread_parts[0], "row", axis=0, tiled=True),
            lax.all_gather(spread_parts[1], "row", axis=0, tiled=True),
        ),
        jnp.int32(0),
    )
    highest, denominator, accumulated = final
    mixed = accumulated.reshape(query_total, HEADS, HEAD_DIM) / denominator.T[:, :, None]
    attended = mixed.reshape(query_total, channels).astype(jnp.bfloat16)
    residual = flattened.astype(jnp.float32) + jnp.dot(
        attended, w_out, preferred_element_type=jnp.float32
    )
    mean_square = jnp.mean(residual * residual, axis=-1, keepdims=True)
    normed = (residual * lax.rsqrt(mean_square + 1e-06) * norm_gain).astype(jnp.bfloat16)
    normed = normed.reshape(frame_count, row_count, channels)
    padded = extended(normed, (("frame", 0),), 1)
    hidden = jax.nn.silu(temporal_mix(padded, w_first, frame_count)).astype(jnp.bfloat16)
    hidden = hidden.reshape(frame_count, row_count, channels)
    padded = extended(hidden, (("frame", 0),), 1)
    second = temporal_mix(padded, w_second, frame_count)
    return (residual + second).astype(jnp.bfloat16).reshape(frame_count, row_count, channels)


def solution(mesh):
    return jax.shard_map(
        shards,
        mesh=mesh,
        in_specs=(P(("clips", "frame"), "row", None), P("clips"), P(), P(), P(), P(), P(), P()),
        out_specs=P(("clips", "frame"), "row", None),
        check_vma=False,
    )
```

profile of v0, /device:TPU:1, one launch (start us, length us, event | category | flops | bytes accessed | tf_op | source)
XLA Modules:
  0.0 162.4 jit_solution(13678371207064377667)
XLA Ops:
  6.5 0.0 copy-start
  6.5 0.0 all-reduce.3.cloned.1.call-start
  6.5 0.8 and_select_fusion.1
  7.3 0.6 fusion.42
  9.2 1.6 gather_fusion
  10.8 0.0 copy-done
  10.8 0.0 copy-start.1
  10.8 0.0 copy-start.5
  10.8 0.7 convolution_convert_fusion
  11.5 0.9 slice_select_fusion
  12.4 0.0 all-reduce.3.cloned.1.call-update
  12.5 0.0 all-gather.3.cloned.1.call-start
  12.5 34.7 %all-reduce.3.cloned.1.call-done = (bf16[128,1280]{1,0:T(8,128)(2,1)}, bf16[128,1280]{1,0:T(8,128)(2,1)}) async-done(((bf16[128,1280]{1,0:T(8,128)(2,1)}, bf16[128,1280]{1,0:T(8,128)(2,1)}), (bf16[128,1280]{1,0:T(8,128)(2,1)}, bf16[128,1280]{1,0:T(8,128)(2,1)})) %all-reduce.3.cloned.1.call-update) | async-done | bytes 655376 | tf_op jit(solution)/shard_map/psum | solution.py:13
  47.2 0.0 all-gather.3.cloned.1.call-update
  47.2 0.0 all-gather.5.cloned.1.call-start
  47.3 0.7 all-gather.5.cloned.1.call-update
  48.0 0.0 copy-done.1
  48.0 0.0 copy-done.5
  48.0 0.5 convolution_convert_fusion.1
  48.4 0.9 copy.12
  49.4 32.9 %all-gather.3.cloned.1.call-done = bf16[512,1280]{1,0:T(8,128)(2,1)} async-done(((bf16[128,1280]{1,0:T(8,128)(2,1)}), bf16[512,1280]{1,0:T(8,128)(2,1)}) %all-gather.3.cloned.1.call-update) | async-done | bytes 1310736 | tf_op jit(solution)/shard_map/all_gather | solution.py:83
  82.2 2.5 %constant_dynamic-update-slice_fusion.1 = bf16[1024,1280]{1,0:T(8,128)(2,1)} fusion(bf16[512,1280]{1,0:T(8,128)(2,1)} %all-gather.3.cloned.1.call-done), kind=kLoop, calls=%fused_computation.54 | loop fusion | bytes 2621440
  84.7 30.8 %all-gather.5.cloned.1.call-done = bf16[512,1280]{1,0:T(8,128)(2,1)} async-done(((bf16[128,1280]{1,0:T(8,128)(2,1)}), bf16[512,1280]{1,0:T(8,128)(2,1)}) %all-gather.5.cloned.1.call-update) | async-done | bytes 1310736 | tf_op jit(solution)/shard_map/all_gather | solution.py:84
  115.5 2.5 %constant_dynamic-update-slice_fusion = bf16[1024,1280]{1,0:T(8,128)(2,1)} fusion(bf16[1024,1280]{1,0:T(8,128)(2,1)} %constant_dynamic-update-slice_fusion.1, bf16[512,1280]{1,0:T(8,128)(2,1)} %all-gather.5.cloned.1.call-done), kind=kLoop, calls=%fused_computation.53 | loop fusion | bytes 2621440 | tf_op jit(solution)/shard_map/concatenate | solution.py:39
  118.0 3.5 %fusion.41 = (bf16[1024,640]{1,0:T(8,128)(2,1)}, bf16[1024,640]{1,0:T(8,128)(2,1)}) fusion(bf16[1024,1280]{1,0:T(8,128)(2,1)} %constant_dynamic-update-slice_fusion), kind=kLoop, calls=%fused_computation.63 | loop fusion | bytes 5242880 | tf_op jit(solution)/shard_map/slice | solution.py:40
  121.5 1.6 copy.13
  123.1 2.5 %copy.14 = bf16[1024,640]{0,1:T(8,128)(2,1)} copy(bf16[1024,640]{1,0:T(8,128)(2,1)} %get-tuple-element.8) | data formatting | bytes 2621440 | tf_op jit(solution)/shard_map/slice | solution.py:41
  125.5 2.6 %multiply_reduce_fusion = (f32[10,256]{1,0:T(8,128)S(1)}, f32[10,256,1024]{2,1,0:T(8,128)S(1)}) fusion(bf16[256,10,64]{0,2,1:T(8,128)(2,1)} %bitcast.74, bf16[1024,10,64]{0,2,1:T(8,128)(2,1)S(1)} %bitcast.69), kind=kOutput, calls=%fused_computation.2 | convolution fusion | flops 340784640 | bytes 12134400 | tf_op jit(solution)/shard_map/qhd,khd->hqk/dot_general | solution.py:42
  128.2 0.0 copy-start.3
  128.2 2.1 %fusion = f32[10,256]{1,0:T(8,128)S(1)} fusion(f32[10,256,1024]{2,1,0:T(8,128)S(1)} %get-tuple-element.26, f32[10,256]{1,0:T(8,128)S(1)} %get-tuple-element.20), kind=kLoop, calls=%fused_computation.3 | loop fusion | flops 7861760 | bytes 10506240 | tf_op jit(solution)/shard_map/reduce_sum | solution.py:48
  130.2 0.0 copy-done.3
  130.2 0.0 copy-start.6
  130.3 0.0 copy-start.7
  130.3 2.3 %fusion.19 = bf16[256,10,64]{0,2,1:T(8,128)(2,1)S(1)} fusion(bf16[1024,10,64]{0,2,1:T(8,128)(2,1)S(1)} %bitcast.77, f32[10,256,1024]{2,1,0:T(8,128)S(1)} %get-tuple-element.26, f32[10,256]{1,0:T(8,128)S(1)} %get-tuple-element.20, f32[256,10]{0,1:T(8,128)S(1)} %bitcast.82, f32[256,10]{0,1:T(8,128)S(1)} %get-tuple-element.19), kind=kOutput, calls=%fused_computation.20 | convolution fusion | flops 343900160 | bytes 12154880 | tf_op jit(solution)/shard_map/hqk,khd->qhd/dot_general | solution.py:49
  132.6 0.0 copy-start.4
  132.6 0.0 copy-done.6
  132.6 0.6 multiply_reduce_fusion.1
  133.2 0.0 copy-done.7
  133.2 0.1 multiply_convert_fusion.1
  133.4 4.3 %collective-permute-start = (bf16[1,128,640]{2,1,0:T(8,128)(2,1)S(1)}, bf16[1,128,640]{2,1,0:T(8,128)(2,1)S(1)}, u32[]{:S(2)}, u32[]{:S(2)}) collective-permute-start(bf16[1,128,640]{2,1,0:T(8,128)(2,1)S(1)} %get-tuple-element.17), channel_id=1, source_target_pairs={{0,4},{4,8},{8,12},{1,5},{5,9},{9,13},{2,6},{6,10},{10,14},{3,7},{... | collective-permute-start | bytes 491528 | tf_op jit(solution)/shard_map/ppermute | solution.py:23
  137.7 1.9 %collective-permute-start.1 = (bf16[1,128,640]{2,1,0:T(8,128)(2,1)S(1)}, bf16[1,128,640]{2,1,0:T(8,128)(2,1)S(1)}, u32[]{:S(2)}, u32[]{:S(2)}) collective-permute-start(bf16[1,128,640]{2,1,0:T(8,128)(2,1)S(1)} %get-tuple-element.18), channel_id=1, source_target_pairs={{4,0},{8,4},{12,8},{5,1},{9,5},{13,9},{6,2},{10,6},{14,10},{7,3},{... | collective-permute-start | bytes 491528 | tf_op jit(solution)/shard_map/ppermute | solution.py:24
  139.6 0.0 copy-done.4
  139.6 0.5 fusion.29
  140.1 0.0 collective-permute-done
  140.1 4.2 %collective-permute-done.1 = bf16[1,128,640]{2,1,0:T(8,128)(2,1)S(1)} collective-permute-done((bf16[1,128,640]{2,1,0:T(8,128)(2,1)S(1)}, bf16[1,128,640]{2,1,0:T(8,128)(2,1)S(1)}, u32[]{:S(2)}, u32[]{:S(2)}) %collective-permute-start.1) | collective-permute-done | bytes 163872 | tf_op jit(solution)/shard_map/ppermute | solution.py:24
  144.3 0.1 pad_maximum_fusion.3
  144.4 0.5 fusion.27
  144.9 0.0 copy-start.2
  144.9 0.5 multiply_convert_fusion
  145.4 2.1 %collective-permute-start.2 = (bf16[1,128,640]{2,1,0:T(8,128)(2,1)S(1)}, bf16[1,128,640]{2,1,0:T(8,128)(2,1)S(1)}, u32[]{:S(2)}, u32[]{:S(2)}) collective-permute-start(bf16[1,128,640]{2,1,0:T(8,128)(2,1)S(1)} %get-tuple-element.13), channel_id=1, source_target_pairs={{0,4},{4,8},{8,12},{1,5},{5,9},{9,13},{2,6},{6,10},{10,14},{3,7},{... | collective-permute-start | bytes 491528 | tf_op jit(solution)/shard_map/ppermute | solution.py:23
  147.5 2.4 %collective-permute-start.3 = (bf16[1,128,640]{2,1,0:T(8,128)(2,1)S(1)}, bf16[1,128,640]{2,1,0:T(8,128)(2,1)S(1)}, u32[]{:S(2)}, u32[]{:S(2)}) collective-permute-start(bf16[1,128,640]{2,1,0:T(8,128)(2,1)S(1)} %get-tuple-element.14), channel_id=1, source_target_pairs={{4,0},{8,4},{12,8},{5,1},{9,5},{13,9},{6,2},{10,6},{14,10},{7,3},{... | collective-permute-start | bytes 491528 | tf_op jit(solution)/shard_map/ppermute | solution.py:24
  149.9 0.0 copy-done.2
  149.9 0.5 fusion.24
  150.4 0.0 collective-permute-done.2
  150.4 3.7 %collective-permute-done.3 = bf16[1,128,640]{2,1,0:T(8,128)(2,1)S(1)} collective-permute-done((bf16[1,128,640]{2,1,0:T(8,128)(2,1)S(1)}, bf16[1,128,640]{2,1,0:T(8,128)(2,1)S(1)}, u32[]{:S(2)}, u32[]{:S(2)}) %collective-permute-start.3) | collective-permute-done | bytes 163872 | tf_op jit(solution)/shard_map/ppermute | solution.py:24
  154.1 0.1 pad_maximum_fusion.1
  154.2 0.5 fusion.22
  154.7 1.2 fusion.15
  (5 shorter events, 0.1 us)
Async XLA Ops:
  6.5 4.3 %copy-start = (bf16[640,1280]{1,0:T(8,128)(2,1)S(1)}, bf16[640,1280]{1,0:T(8,128)(2,1)}, u32[]{:S(2)}) copy-start(bf16[640,1280]{1,0:T(8,128)(2,1)} %param.11) | copy-start | bytes 4915204
  6.5 40.7 %all-reduce.3.cloned.1.call-start = ((), (), s32[]{:S(2)}) async-start(), calls=%async_computation.2 | async-start | bytes 1310720 | tf_op jit(solution)/shard_map/psum | solution.py:13
  10.8 37.2 %copy-start.1 = (bf16[2,128,640]{2,1,0:T(8,128)(2,1)S(1)}, bf16[2,128,640]{2,1,0:T(8,128)(2,1)}, u32[]{:S(2)}) copy-start(bf16[2,128,640]{2,1,0:T(8,128)(2,1)} %param.8) | copy-start | bytes 983044
  10.8 37.2 %copy-start.5 = (bf16[640,640]{1,0:T(8,128)(2,1)S(1)}, bf16[640,640]{1,0:T(8,128)(2,1)}, u32[]{:S(2)}) copy-start(bf16[640,640]{1,0:T(8,128)(2,1)} %param.10) | copy-start | bytes 2457604
  12.5 69.8 %all-gather.3.cloned.1.call-start = ((), (), s32[]{:S(2)}) async-start(), calls=%async_computation | async-start | bytes 1638400 | tf_op jit(solution)/shard_map/all_gather | solution.py:83
  47.2 68.3 %all-gather.5.cloned.1.call-start = ((), (), s32[]{:S(2)}) async-start(), calls=%async_computation.1 | async-start | bytes 1638400 | tf_op jit(solution)/shard_map/all_gather | solution.py:84
  128.2 2.1 %copy-start.3 = (bf16[1024,640]{0,1:T(8,128)(2,1)S(1)}, bf16[1024,640]{0,1:T(8,128)(2,1)}, u32[]{:S(2)}) copy-start(bf16[1024,640]{0,1:T(8,128)(2,1)} %copy.14) | copy-start | bytes 3932164
  130.2 2.3 %copy-start.6 = (bf16[640,640]{1,0:T(8,128)(2,1)S(1)}, bf16[640,640]{1,0:T(8,128)(2,1)}, u32[]{:S(2)}) copy-start(bf16[640,640]{1,0:T(8,128)(2,1)} %param.12) | copy-start | bytes 2457604
  130.3 2.9 %copy-start.7 = (f32[640]{0:T(1024)S(1)}, f32[640]{0:T(1024)}, u32[]{:S(2)}) copy-start(f32[640]{0:T(1024)} %param.13) | copy-start | bytes 7684
  132.6 7.1 %copy-start.4 = (bf16[3,640,640]{2,1,0:T(8,128)(2,1)S(1)}, bf16[3,640,640]{2,1,0:T(8,128)(2,1)}, u32[]{:S(2)}) copy-start(bf16[3,640,640]{2,1,0:T(8,128)(2,1)} %param.14) | copy-start | bytes 7372804
  133.4 6.7 %collective-permute-start = (bf16[1,128,640]{2,1,0:T(8,128)(2,1)S(1)}, bf16[1,128,640]{2,1,0:T(8,128)(2,1)S(1)}, u32[]{:S(2)}, u32[]{:S(2)}) collective-permute-start(bf16[1,128,640]{2,1,0:T(8,128)(2,1)S(1)} %get-tuple-element.17), channel_id=1, source_target_pairs={{0,4},{4,8},{8,12},{1,5},{5,9},{9,13},{2,6},{6,10},{10,14},{3,7},{... | collective-permute-start | bytes 491528 | tf_op jit(solution)/shard_map/ppermute | solution.py:23
  137.7 6.6 %collective-permute-start.1 = (bf16[1,128,640]{2,1,0:T(8,128)(2,1)S(1)}, bf16[1,128,640]{2,1,0:T(8,128)(2,1)S(1)}, u32[]{:S(2)}, u32[]{:S(2)}) collective-permute-start(bf16[1,128,640]{2,1,0:T(8,128)(2,1)S(1)} %get-tuple-element.18), channel_id=1, source_target_pairs={{4,0},{8,4},{12,8},{5,1},{9,5},{13,9},{6,2},{10,6},{14,10},{7,3},{... | collective-permute-start | bytes 491528 | tf_op jit(solution)/shard_map/ppermute | solution.py:24
  144.9 5.1 %copy-start.2 = (bf16[3,640,640]{2,1,0:T(8,128)(2,1)S(1)}, bf16[3,640,640]{2,1,0:T(8,128)(2,1)}, u32[]{:S(2)}) copy-start(bf16[3,640,640]{2,1,0:T(8,128)(2,1)} %param.15) | copy-start | bytes 7372804
  145.4 5.0 %collective-permute-start.2 = (bf16[1,128,640]{2,1,0:T(8,128)(2,1)S(1)}, bf16[1,128,640]{2,1,0:T(8,128)(2,1)S(1)}, u32[]{:S(2)}, u32[]{:S(2)}) collective-permute-start(bf16[1,128,640]{2,1,0:T(8,128)(2,1)S(1)} %get-tuple-element.13), channel_id=1, source_target_pairs={{0,4},{4,8},{8,12},{1,5},{5,9},{9,13},{2,6},{6,10},{10,14},{3,7},{... | collective-permute-start | bytes 491528 | tf_op jit(solution)/shard_map/ppermute | solution.py:23
  147.5 6.6 %collective-permute-start.3 = (bf16[1,128,640]{2,1,0:T(8,128)(2,1)S(1)}, bf16[1,128,640]{2,1,0:T(8,128)(2,1)S(1)}, u32[]{:S(2)}, u32[]{:S(2)}) collective-permute-start(bf16[1,128,640]{2,1,0:T(8,128)(2,1)S(1)} %get-tuple-element.14), channel_id=1, source_target_pairs={{4,0},{8,4},{12,8},{5,1},{9,5},{13,9},{6,2},{10,6},{14,10},{7,3},{... | collective-permute-start | bytes 491528 | tf_op jit(solution)/shard_map/ppermute | solution.py:24
Sparse Core Ops, SparseCore 0:
  12.6 34.5 all-reduce.2
  48.8 33.4 all-gather.2
  83.8 31.6 all-gather.4
where the time goes:
time: 163 us; the launch traced here: 162 us
  waiting for transfers between devices  107 us (66%)
  local copies, waits for them, and re-layouts  15.6 us (10%)
  between operations  14.7 us (9%)
  starting transfers between devices  10.8 us (7%)
  matrix products  10.2 us (6%)
  other arithmetic  4.05 us (2%)
    psum x1, waiting for transfers between devices, from_root(): return lax.psum(kept, axis)  34.7 us
    all_gather x1, waiting for transfers between devices, shards(): lax.all_gather(spread_parts[0], 'row', axis=0, tiled=True)  32.9 us
    all_gather x1, waiting for transfers between devices, shards(): lax.all_gather(spread_parts[1], 'row', axis=0, tiled=True)  30.8 us
    ppermute x2, waiting for transfers between devices, extended(): after = lax.ppermute(first, axis, down)  7.96 us
    ppermute x2, starting transfers between devices, extended(): before = lax.ppermute(last, axis, up)  6.37 us
    slice x2, local copies, waits for them, and re-layouts, absorb_keys(): key_heads = joined[:, :channels].reshape(-1, HEADS, HEAD_DIM)  5.06 us
    ppermute x2, starting transfers between devices, extended(): after = lax.ppermute(first, axis, down)  4.33 us
    dot_general x6, matrix products, temporal_mix(): jnp.dot(window, weights[offset], preferred_element_type=jnp.float32)  3.53 us
  transfers between devices with their start and end apart: 7, of which 5 were waited for; matrix products, arithmetic and copies ran while one was open for 3% of the time, Pallas kernels for 0%

commit v1 on v0

--- a/solution.py
+++ b/solution.py
@@ -6,6 +6,24 @@
 
 HEADS = 10
 HEAD_DIM = 64
+
+
+def collect(value, axis, dim):
+    ways, here, step = (lax.axis_size(axis), lax.axis_index(axis), value.shape[dim])
+    shape = [n * ways if d == dim else n for d, n in enumerate(value.shape)]
+    full = lax.dynamic_update_slice_in_dim(
+        jnp.zeros(shape, value.dtype), value, here * step, axis=dim
+    )
+    going_up = going_down = value
+    for far in range(1, ways // 2 + 1):
+        going_up = lax.ppermute(going_up, axis, [(d, (d + 1) % ways) for d in range(ways)])
+        full = lax.dynamic_update_slice_in_dim(full, going_up, (here - far) % ways * step, axis=dim)
+        if 2 * far < ways:
+            going_down = lax.ppermute(going_down, axis, [(d, (d - 1) % ways) for d in range(ways)])
+            full = lax.dynamic_update_slice_in_dim(
+                full, going_down, (here + far) % ways * step, axis=dim
+            )
+    return full
 
 
 def from_root(value, axis, source):
@@ -80,7 +98,7 @@
     final = absorb(
         initial,
         (
-            lax.all_gather(spread_parts[0], "row", axis=0, tiled=True),
+            collect(spread_parts[0], "row", 0),
             lax.all_gather(spread_parts[1], "row", axis=0, tiled=True),
         ),
         jnp.int32(0),

time: 163 us -> 138 us (0.85)
  waiting for transfers between devices: 107 us -> 82.9 us
  local copies, waits for them, and re-layouts: 15.6 us -> 9.45 us
  other arithmetic: 4.05 us -> 7 us
  starting transfers between devices: 10.8 us -> 13.2 us
    all_gather x1 -> x0, waiting for transfers between devices: 32.9 us -> none  [shards(): lax.all_gather(spread_parts[0], 'row', axis=0, tiled=True)]
    ppermute x0 -> x3, waiting for transfers between devices: none -> 26.2 us  [the longest x1 22.5 us: collect(): lax.ppermute(going_down, axis, [(d, (d - 1) % ways) for d in range(ways)])]
    all_gather x1, waiting for transfers between devices: 30.8 us -> 14 us  [shards(): lax.all_gather(spread_parts[1], 'row', axis=0, tiled=True)]
    ppermute x0 -> x3, starting transfers between devices: none -> 3.62 us  [the longest x1 1.87 us: collect(): lax.ppermute(going_down, axis, [(d, (d - 1) % ways) for d in range(ways)])]
    slice x2 -> x1, local copies, waits for them, and re-layouts: 5.06 us -> 1.6 us  [absorb_keys(): key_heads = joined[:, :channels].reshape(-1, HEADS, HEAD_DIM)]
    concatenate x0 -> x1, other arithmetic: none -> 2.98 us  [absorb_keys(): joined = jnp.concatenate(kv_pieces, axis=0)]
    unnamed x17 -> x16, local copies, waits for them, and re-layouts: 2.52 us -> 0.05 us
    concatenate x1 -> x0, local copies, waits for them, and re-layouts: 2.46 us -> none  [absorb_keys(): joined = jnp.concatenate(kv_pieces, axis=0)]
  transfers between devices with their start and end apart: 7 -> 9, of which waited for: 5 -> 6; matrix products, arithmetic and copies ran while one was open for 3% -> 3% of each run, Pallas kernels for 0% -> 0%
where the time goes in v1:
time: 138 us
  waiting for transfers between devices  82.9 us (60%)
  between operations  15 us (11%)
  starting transfers between devices  13.2 us (10%)
  matrix products  10.2 us (7%)
  local copies, waits for them, and re-layouts  9.45 us (7%)
  other arithmetic  7 us (5%)
    psum x1, waiting for transfers between devices, from_root(): return lax.psum(kept, axis)  34.7 us
    ppermute x1, waiting for transfers between devices, collect(): lax.ppermute(going_down, axis, [(d, (d - 1) % ways) for d in range(ways)])  22.5 us
    all_gather x1, waiting for transfers between devices, shards(): lax.all_gather(spread_parts[1], 'row', axis=0, tiled=True)  14 us
    ppermute x2, waiting for transfers between devices, extended(): after = lax.ppermute(first, axis, down)  7.96 us
    ppermute x2, starting transfers between devices, extended(): before = lax.ppermute(last, axis, up)  5.2 us
    ppermute x2, starting transfers between devices, extended(): after = lax.ppermute(first, axis, down)  4.33 us
    ppermute x2, waiting for transfers between devices, collect(): lax.ppermute(going_up, axis, [(d, (d + 1) % ways) for d in range(ways)])  3.76 us
    dot_general x6, matrix products, temporal_mix(): jnp.dot(window, weights[offset], preferred_element_type=jnp.float32)  3.53 us
  transfers between devices with their start and end apart: 9, of which 6 were waited for; matrix products, arithmetic and copies ran while one was open for 3% of the time, Pallas kernels for 0%

profile of v1, /device:TPU:1, one launch (start us, length us, event | category | flops | bytes accessed | tf_op | source)
XLA Modules:
  0.0 137.8 jit_solution(853758454877228658)
XLA Ops:
  6.5 0.0 copy-start
  6.5 0.0 all-reduce.3.cloned.1.call-start
  6.5 0.8 and_select_fusion.1
  7.3 0.6 fusion.42
  9.2 1.6 %gather_fusion = bf16[2,128,640]{2,1,0:T(8,128)(2,1)S(1)} fusion(bf16[2,128,640]{2,1,0:T(8,128)(2,1)} %param.8, s32[1024]{0:T(1024)S(1)} %pad_clamp_fusion), kind=kCustom, calls=%fused_computation | custom fusion | bytes 655368 | tf_op jit(solution)/shard_map/gather | solution.py:86
  10.8 0.0 copy-done
  10.8 0.0 copy-start.1
  10.9 0.0 copy-start.5
  10.9 0.7 convolution_convert_fusion
  11.6 0.9 slice_select_fusion.1
  12.4 0.0 all-reduce.3.cloned.1.call-update
  12.5 0.0 all-gather.2.cloned.1.call-start
  12.5 34.7 %all-reduce.3.cloned.1.call-done = (bf16[128,1280]{1,0:T(8,128)(2,1)}, bf16[128,1280]{1,0:T(8,128)(2,1)}) async-done(((bf16[128,1280]{1,0:T(8,128)(2,1)}, bf16[128,1280]{1,0:T(8,128)(2,1)}), (bf16[128,1280]{1,0:T(8,128)(2,1)}, bf16[128,1280]{1,0:T(8,128)(2,1)})) %all-reduce.3.cloned.1.call-update) | async-done | bytes 655376 | tf_op jit(solution)/shard_map/psum | solution.py:31
  47.2 0.0 all-gather.2.cloned.1.call-update
  47.2 1.7 %collective-permute-start = (bf16[128,1280]{1,0:T(8,128)(2,1)}, bf16[128,1280]{1,0:T(8,128)(2,1)}, u32[]{:S(2)}, u32[]{:S(2)}) collective-permute-start(bf16[128,1280]{1,0:T(8,128)(2,1)} %get-tuple-element.6), channel_id=1, source_target_pairs={{0,1},{1,2},{2,3},{3,0},{4,5},{5,6},{6,7},{7,4},{8,9},{9,10},{10,1... | collective-permute-start | bytes 983048 | tf_op jit(solution)/shard_map/ppermute | solution.py:19
  49.0 0.0 copy-done.1
  49.0 0.0 copy-done.5
  49.0 0.5 convolution_convert_fusion.1
  49.5 0.9 copy.12
  50.4 1.9 %collective-permute-start.1 = (bf16[128,1280]{1,0:T(8,128)(2,1)}, bf16[128,1280]{1,0:T(8,128)(2,1)S(1)}, u32[]{:S(2)}, u32[]{:S(2)}) collective-permute-start(bf16[128,1280]{1,0:T(8,128)(2,1)} %get-tuple-element.6), channel_id=1, source_target_pairs={{0,3},{1,0},{2,1},{3,2},{4,7},{5,4},{6,5},{7,6},{8,11},{9,8},{10,9... | collective-permute-start | bytes 983048 | tf_op jit(solution)/shard_map/ppermute | solution.py:22
  52.3 0.1 broadcast_in_dim.25
  52.4 1.0 constant_dynamic-update-slice_fusion.3
  53.4 3.8 %collective-permute-done = bf16[128,1280]{1,0:T(8,128)(2,1)} collective-permute-done((bf16[128,1280]{1,0:T(8,128)(2,1)}, bf16[128,1280]{1,0:T(8,128)(2,1)}, u32[]{:S(2)}, u32[]{:S(2)}) %collective-permute-start) | collective-permute-done | bytes 327712 | tf_op jit(solution)/shard_map/ppermute | solution.py:19
  57.1 0.0 collective-permute-start.2
  57.1 1.0 constant_dynamic-update-slice_fusion.2
  58.2 22.5 %collective-permute-done.1 = bf16[128,1280]{1,0:T(8,128)(2,1)S(1)} collective-permute-done((bf16[128,1280]{1,0:T(8,128)(2,1)}, bf16[128,1280]{1,0:T(8,128)(2,1)S(1)}, u32[]{:S(2)}, u32[]{:S(2)}) %collective-permute-start.1) | collective-permute-done | bytes 327712 | tf_op jit(solution)/shard_map/ppermute | solution.py:22
  80.7 0.0 collective-permute-done.2
  80.7 14.0 %all-gather.2.cloned.1.call-done = bf16[512,1280]{1,0:T(8,128)(2,1)} async-done(((bf16[128,1280]{1,0:T(8,128)(2,1)}), bf16[512,1280]{1,0:T(8,128)(2,1)}) %all-gather.2.cloned.1.call-update) | async-done | bytes 1310736 | tf_op jit(solution)/shard_map/all_gather | solution.py:102
  94.7 3.0 %fusion.6 = (bf16[1024,640]{1,0:T(8,128)(2,1)}, bf16[1024,640]{1,0:T(8,128)(2,1)}) fusion(bf16[512,1280]{1,0:T(8,128)(2,1)S(1)} %constant_dynamic-update-slice_fusion, bf16[512,1280]{1,0:T(8,128)(2,1)} %all-gather.2.cloned.1.call-done), kind=kLoop, calls=%fused_computation.11 | loop fusion | flops 5242880 | bytes 5242880 | tf_op jit(solution)/shard_map/concatenate | solution.py:57
  97.7 1.6 %copy.13 = bf16[1024,640]{0,1:T(8,128)(2,1)S(1)} copy(bf16[1024,640]{1,0:T(8,128)(2,1)} %get-tuple-element.7) | data formatting | bytes 2621440 | tf_op jit(solution)/shard_map/slice | solution.py:58
  99.3 2.5 %copy.14 = bf16[1024,640]{0,1:T(8,128)(2,1)} copy(bf16[1024,640]{1,0:T(8,128)(2,1)} %get-tuple-element.8) | data formatting | bytes 2621440 | tf_op jit(solution)/shard_map/slice | solution.py:59
  101.8 2.6 %multiply_reduce_fusion = (f32[10,256]{1,0:T(8,128)S(1)}, f32[10,256,1024]{2,1,0:T(8,128)S(1)}) fusion(bf16[256,10,64]{0,2,1:T(8,128)(2,1)} %bitcast.74, bf16[1024,10,64]{0,2,1:T(8,128)(2,1)S(1)} %bitcast.69), kind=kOutput, calls=%fused_computation.2 | convolution fusion | flops 340784640 | bytes 12134400 | tf_op jit(solution)/shard_map/qhd,khd->hqk/dot_general | solution.py:60
  104.4 0.0 copy-start.3
  104.4 2.1 %fusion = f32[10,256]{1,0:T(8,128)S(1)} fusion(f32[10,256,1024]{2,1,0:T(8,128)S(1)} %get-tuple-element.26, f32[10,256]{1,0:T(8,128)S(1)} %get-tuple-element.20), kind=kLoop, calls=%fused_computation.3 | loop fusion | flops 7861760 | bytes 10506240 | tf_op jit(solution)/shard_map/reduce_sum | solution.py:66
  106.5 0.0 copy-done.3
  106.5 0.0 copy-start.6
  106.5 0.0 copy-start.7
  106.5 2.3 %fusion.20 = bf16[256,10,64]{0,2,1:T(8,128)(2,1)S(1)} fusion(bf16[1024,10,64]{0,2,1:T(8,128)(2,1)S(1)} %bitcast.77, f32[10,256,1024]{2,1,0:T(8,128)S(1)} %get-tuple-element.26, f32[10,256]{1,0:T(8,128)S(1)} %get-tuple-element.20, f32[256,10]{0,1:T(8,128)S(1)} %bitcast.82, f32[256,10]{0,1:T(8,128)S(1)} %get-tuple-element.19), kind=kOutput, calls=%fused_computation.24 | convolution fusion | flops 343900160 | bytes 12154880 | tf_op jit(solution)/shard_map/hqk,khd->qhd/dot_general | solution.py:67
  108.8 0.0 copy-start.4
  108.9 0.0 copy-done.6
  108.9 0.6 multiply_reduce_fusion.1
  109.5 0.0 copy-done.7
  109.5 0.1 multiply_convert_fusion.1
  109.6 3.1 %collective-permute-start.3 = (bf16[1,128,640]{2,1,0:T(8,128)(2,1)S(1)}, bf16[1,128,640]{2,1,0:T(8,128)(2,1)S(1)}, u32[]{:S(2)}, u32[]{:S(2)}) collective-permute-start(bf16[1,128,640]{2,1,0:T(8,128)(2,1)S(1)} %get-tuple-element.17), channel_id=1, source_target_pairs={{0,4},{4,8},{8,12},{1,5},{5,9},{9,13},{2,6},{6,10},{10,14},{3,7},{... | collective-permute-start | bytes 491528 | tf_op jit(solution)/shard_map/ppermute | solution.py:41
  112.8 1.9 %collective-permute-start.4 = (bf16[1,128,640]{2,1,0:T(8,128)(2,1)S(1)}, bf16[1,128,640]{2,1,0:T(8,128)(2,1)S(1)}, u32[]{:S(2)}, u32[]{:S(2)}) collective-permute-start(bf16[1,128,640]{2,1,0:T(8,128)(2,1)S(1)} %get-tuple-element.18), channel_id=1, source_target_pairs={{4,0},{8,4},{12,8},{5,1},{9,5},{13,9},{6,2},{10,6},{14,10},{7,3},{... | collective-permute-start | bytes 491528 | tf_op jit(solution)/shard_map/ppermute | solution.py:42
  114.7 0.0 copy-done.4
  114.7 0.5 fusion.30
  115.2 0.0 collective-permute-done.3
  115.2 4.2 %collective-permute-done.4 = bf16[1,128,640]{2,1,0:T(8,128)(2,1)S(1)} collective-permute-done((bf16[1,128,640]{2,1,0:T(8,128)(2,1)S(1)}, bf16[1,128,640]{2,1,0:T(8,128)(2,1)S(1)}, u32[]{:S(2)}, u32[]{:S(2)}) %collective-permute-start.4) | collective-permute-done | bytes 163872 | tf_op jit(solution)/shard_map/ppermute | solution.py:42
  119.4 0.1 pad_maximum_fusion.4
  119.5 0.5 fusion.28
  120.0 0.0 copy-start.2
  120.0 0.5 multiply_convert_fusion
  120.5 2.1 %collective-permute-start.5 = (bf16[1,128,640]{2,1,0:T(8,128)(2,1)S(1)}, bf16[1,128,640]{2,1,0:T(8,128)(2,1)S(1)}, u32[]{:S(2)}, u32[]{:S(2)}) collective-permute-start(bf16[1,128,640]{2,1,0:T(8,128)(2,1)S(1)} %get-tuple-element.13), channel_id=1, source_target_pairs={{0,4},{4,8},{8,12},{1,5},{5,9},{9,13},{2,6},{6,10},{10,14},{3,7},{... | collective-permute-start | bytes 491528 | tf_op jit(solution)/shard_map/ppermute | solution.py:41
  122.6 2.4 %collective-permute-start.6 = (bf16[1,128,640]{2,1,0:T(8,128)(2,1)S(1)}, bf16[1,128,640]{2,1,0:T(8,128)(2,1)S(1)}, u32[]{:S(2)}, u32[]{:S(2)}) collective-permute-start(bf16[1,128,640]{2,1,0:T(8,128)(2,1)S(1)} %get-tuple-element.14), channel_id=1, source_target_pairs={{4,0},{8,4},{12,8},{5,1},{9,5},{13,9},{6,2},{10,6},{14,10},{7,3},{... | collective-permute-start | bytes 491528 | tf_op jit(solution)/shard_map/ppermute | solution.py:42
  125.0 0.0 copy-done.2
  125.0 0.5 fusion.25
  125.5 0.0 collective-permute-done.5
  125.5 3.7 %collective-permute-done.6 = bf16[1,128,640]{2,1,0:T(8,128)(2,1)S(1)} collective-permute-done((bf16[1,128,640]{2,1,0:T(8,128)(2,1)S(1)}, bf16[1,128,640]{2,1,0:T(8,128)(2,1)S(1)}, u32[]{:S(2)}, u32[]{:S(2)}) %collective-permute-start.6) | collective-permute-done | bytes 163872 | tf_op jit(solution)/shard_map/ppermute | solution.py:42
  129.2 0.1 pad_maximum_fusion.2
  129.3 0.5 fusion.23
  129.8 1.2 fusion.16
  (7 shorter events, 0.1 us)
Async XLA Ops:
  6.5 4.3 %copy-start = (bf16[640,1280]{1,0:T(8,128)(2,1)S(1)}, bf16[640,1280]{1,0:T(8,128)(2,1)}, u32[]{:S(2)}) copy-start(bf16[640,1280]{1,0:T(8,128)(2,1)} %param.11) | copy-start | bytes 4915204
  6.5 40.7 %all-reduce.3.cloned.1.call-start = ((), (), s32[]{:S(2)}) async-start(), calls=%async_computation.1 | async-start | bytes 1310720 | tf_op jit(solution)/shard_map/psum | solution.py:31
  10.8 38.1 %copy-start.1 = (bf16[2,128,640]{2,1,0:T(8,128)(2,1)S(1)}, bf16[2,128,640]{2,1,0:T(8,128)(2,1)}, u32[]{:S(2)}) copy-start(bf16[2,128,640]{2,1,0:T(8,128)(2,1)} %param.8) | copy-start | bytes 983044
  10.9 38.1 %copy-start.5 = (bf16[640,640]{1,0:T(8,128)(2,1)S(1)}, bf16[640,640]{1,0:T(8,128)(2,1)}, u32[]{:S(2)}) copy-start(bf16[640,640]{1,0:T(8,128)(2,1)} %param.10) | copy-start | bytes 2457604
  12.5 82.3 %all-gather.2.cloned.1.call-start = ((), (), s32[]{:S(2)}) async-start(), calls=%async_computation | async-start | bytes 1638400 | tf_op jit(solution)/shard_map/all_gather | solution.py:102
  47.2 9.9 %collective-permute-start = (bf16[128,1280]{1,0:T(8,128)(2,1)}, bf16[128,1280]{1,0:T(8,128)(2,1)}, u32[]{:S(2)}, u32[]{:S(2)}) collective-permute-start(bf16[128,1280]{1,0:T(8,128)(2,1)} %get-tuple-element.6), channel_id=1, source_target_pairs={{0,1},{1,2},{2,3},{3,0},{4,5},{5,6},{6,7},{7,4},{8,9},{9,10},{10,1... | collective-permute-start | bytes 983048 | tf_op jit(solution)/shard_map/ppermute | solution.py:19
  50.4 30.2 %collective-permute-start.1 = (bf16[128,1280]{1,0:T(8,128)(2,1)}, bf16[128,1280]{1,0:T(8,128)(2,1)S(1)}, u32[]{:S(2)}, u32[]{:S(2)}) collective-permute-start(bf16[128,1280]{1,0:T(8,128)(2,1)} %get-tuple-element.6), channel_id=1, source_target_pairs={{0,3},{1,0},{2,1},{3,2},{4,7},{5,4},{6,5},{7,6},{8,11},{9,8},{10,9... | collective-permute-start | bytes 983048 | tf_op jit(solution)/shard_map/ppermute | solution.py:22
  57.1 23.5 %collective-permute-start.2 = (bf16[128,1280]{1,0:T(8,128)(2,1)}, bf16[128,1280]{1,0:T(8,128)(2,1)S(1)}, u32[]{:S(2)}, u32[]{:S(2)}) collective-permute-start(bf16[128,1280]{1,0:T(8,128)(2,1)} %collective-permute-done), channel_id=1, source_target_pairs={{0,1},{1,2},{2,3},{3,0},{4,5},{5,6},{6,7},{7,4},{8,9},{9,10},{10,1... | collective-permute-start | bytes 983048 | tf_op jit(solution)/shard_map/ppermute | solution.py:19
  104.4 2.1 %copy-start.3 = (bf16[1024,640]{0,1:T(8,128)(2,1)S(1)}, bf16[1024,640]{0,1:T(8,128)(2,1)}, u32[]{:S(2)}) copy-start(bf16[1024,640]{0,1:T(8,128)(2,1)} %copy.14) | copy-start | bytes 3932164
  106.5 2.4 %copy-start.6 = (bf16[640,640]{1,0:T(8,128)(2,1)S(1)}, bf16[640,640]{1,0:T(8,128)(2,1)}, u32[]{:S(2)}) copy-start(bf16[640,640]{1,0:T(8,128)(2,1)} %param.12) | copy-start | bytes 2457604
  106.5 2.9 %copy-start.7 = (f32[640]{0:T(1024)S(1)}, f32[640]{0:T(1024)}, u32[]{:S(2)}) copy-start(f32[640]{0:T(1024)} %param.13) | copy-start | bytes 7684
  108.8 5.9 %copy-start.4 = (bf16[3,640,640]{2,1,0:T(8,128)(2,1)S(1)}, bf16[3,640,640]{2,1,0:T(8,128)(2,1)}, u32[]{:S(2)}) copy-start(bf16[3,640,640]{2,1,0:T(8,128)(2,1)} %param.14) | copy-start | bytes 7372804
  109.6 5.6 %collective-permute-start.3 = (bf16[1,128,640]{2,1,0:T(8,128)(2,1)S(1)}, bf16[1,128,640]{2,1,0:T(8,128)(2,1)S(1)}, u32[]{:S(2)}, u32[]{:S(2)}) collective-permute-start(bf16[1,128,640]{2,1,0:T(8,128)(2,1)S(1)} %get-tuple-element.17), channel_id=1, source_target_pairs={{0,4},{4,8},{8,12},{1,5},{5,9},{9,13},{2,6},{6,10},{10,14},{3,7},{... | collective-permute-start | bytes 491528 | tf_op jit(solution)/shard_map/ppermute | solution.py:41
  112.8 6.6 %collective-permute-start.4 = (bf16[1,128,640]{2,1,0:T(8,128)(2,1)S(1)}, bf16[1,128,640]{2,1,0:T(8,128)(2,1)S(1)}, u32[]{:S(2)}, u32[]{:S(2)}) collective-permute-start(bf16[1,128,640]{2,1,0:T(8,128)(2,1)S(1)} %get-tuple-element.18), channel_id=1, source_target_pairs={{4,0},{8,4},{12,8},{5,1},{9,5},{13,9},{6,2},{10,6},{14,10},{7,3},{... | collective-permute-start | bytes 491528 | tf_op jit(solution)/shard_map/ppermute | solution.py:42
  120.0 5.1 %copy-start.2 = (bf16[3,640,640]{2,1,0:T(8,128)(2,1)S(1)}, bf16[3,640,640]{2,1,0:T(8,128)(2,1)}, u32[]{:S(2)}) copy-start(bf16[3,640,640]{2,1,0:T(8,128)(2,1)} %param.15) | copy-start | bytes 7372804
  120.5 5.0 %collective-permute-start.5 = (bf16[1,128,640]{2,1,0:T(8,128)(2,1)S(1)}, bf16[1,128,640]{2,1,0:T(8,128)(2,1)S(1)}, u32[]{:S(2)}, u32[]{:S(2)}) collective-permute-start(bf16[1,128,640]{2,1,0:T(8,128)(2,1)S(1)} %get-tuple-element.13), channel_id=1, source_target_pairs={{0,4},{4,8},{8,12},{1,5},{5,9},{9,13},{2,6},{6,10},{10,14},{3,7},{... | collective-permute-start | bytes 491528 | tf_op jit(solution)/shard_map/ppermute | solution.py:41
  122.6 6.6 %collective-permute-start.6 = (bf16[1,128,640]{2,1,0:T(8,128)(2,1)S(1)}, bf16[1,128,640]{2,1,0:T(8,128)(2,1)S(1)}, u32[]{:S(2)}, u32[]{:S(2)}) collective-permute-start(bf16[1,128,640]{2,1,0:T(8,128)(2,1)S(1)} %get-tuple-element.14), channel_id=1, source_target_pairs={{4,0},{8,4},{12,8},{5,1},{9,5},{13,9},{6,2},{10,6},{14,10},{7,3},{... | collective-permute-start | bytes 491528 | tf_op jit(solution)/shard_map/ppermute | solution.py:42
Sparse Core Ops, SparseCore 0:
  12.6 34.5 all-reduce.2
  48.8 45.9 all-gather.1
